TPU v7x, 512 devices: a whole 4x8x8 slice. The times are simulated.
512 devices in a mesh: section: 32 (over z, x), neuron: 16 (over y, core).
Axes of the slice: x: 4, y: 8, z: 8, core: 2. Of those that a mesh axis runs over, the one named last changes fastest.
Arguments:
- inputs: bfloat16 [6, 32768], P(None, 'neuron'), may hold values from 0 to 2
- weight_tiles: bfloat16 [32, 2048, 128, 128], P('section', 'neuron'), may hold values from -0.07324219 to 0.07910156
- source_block: int32 [32, 2048], P('section', 'neuron'), may hold values from 0 to 255
- target_block: int32 [32, 2048], P('section', 'neuron'), may hold values from 0 to 15
- live_slots: int32 [32, 16], P('section', 'neuron'), may hold values from 16 to 128, as said below
Outputs:
- activations: bfloat16 [32, 6, 32768], P('section', None, 'neuron')
Inputs may be any that keep to these rules, and one draw needn't show every extreme that they name: live_slots[l, n] is 128, 64, 32 or 16, and in every layer some shard has all 128 slots live.
All inputs are finite; a program needn't handle non-finite values.
Results may differ from a plain program's by a relative error of at most 0.0045.
Values may be sent and summed in bfloat16 or wider, within the bound.
No kernel may reach another device: no remote copies, remote signals or barrier semaphores. Data moves between devices by JAX's collectives and lax.ppermute only.
A program may use at most 64 MiB of HBM per device.

v0:
```python
import jax
import jax.numpy as jnp
from jax import lax
from jax.sharding import PartitionSpec as P

NEURON_BIAS = -0.3
CLIP_LEVEL = 32.0
UNROLL = True


def layer_apply(gathered, weight_tiles, source, selector):
    row_count = gathered.shape[0]
    block_size = weight_tiles.shape[2]
    column_count = selector.shape[1]
    block_count = gathered.shape[1] // block_size
    shaped = gathered.reshape(row_count, block_count, block_size)
    picked = shaped.at[:, source].get(mode="promise_in_bounds")
    partial_value = jnp.einsum(
        "msk,skj->msj", picked, weight_tiles[0], preferred_element_type=jnp.float32
    )
    summed = jnp.einsum(
        "msj,sc->mcj", partial_value, selector, precision=lax.Precision.HIGHEST
    )
    result = jnp.clip(summed + NEURON_BIAS, 0.0, CLIP_LEVEL).astype(jnp.bfloat16)
    return result.reshape(row_count, column_count * block_size)


def local(inputs, weight_tiles, source_block, target_block, live_slots):
    section_pos = lax.axis_index("section")
    section_count = lax.axis_size("section")
    row_count, shard_width = inputs.shape
    slot_count = weight_tiles.shape[1]
    column_count = shard_width // weight_tiles.shape[2]

    source = source_block[0]
    live_mask = jnp.arange(slot_count, dtype=jnp.int32) < live_slots[0, 0]
    selector = (
        (target_block[0][:, None] == jnp.arange(column_count, dtype=jnp.int32)[None, :])
        & live_mask[:, None]
    ).astype(jnp.float32)

    def compute(gathered):
        return layer_apply(gathered, weight_tiles, source, selector)

    def empty(gathered):
        return jnp.zeros((row_count, shard_width), jnp.bfloat16)

    def step(step_num, current, collected, route):
        gathered = lax.all_gather(current, "neuron", axis=1, tiled=True)
        active = section_pos == step_num
        result = lax.cond(active, compute, empty, gathered)
        collected = jnp.where(active, result, collected)
        if route is None:
            return result, collected
        return lax.ppermute(result, "section", route), collected

    collected = jnp.zeros((row_count, shard_width), jnp.bfloat16)
    current = inputs
    if UNROLL:
        for t in range(section_count - 1):
            current, collected = step(t, current, collected, [(t, t + 1)])
    else:
        route = [(i, i + 1) for i in range(section_count - 1)]
        current, collected = lax.fori_loop(
            0, section_count - 1, lambda t, c: step(t, c[0], c[1], route), (current, collected)
        )
    _, collected = step(section_count - 1, current, collected, None)
    return collected[None]


def solution(mesh):
    in_specs = (
        P(None, "neuron"),
        P("section", "neuron", None, None),
        P("section", "neuron"),
        P("section", "neuron"),
        P("section", "neuron"),
    )
    out_specs = P("section", None, "neuron")
    return jax.shard_map(local, mesh=mesh, in_specs=in_specs, out_specs=out_specs, check_vma=False)
```

profile of v0, /device:TPU:455, one launch (start us, length us, event | category | flops | bytes accessed | tf_op | source)
XLA Modules:
  0.0 831.7 jit_solution(17067444347415175428)
XLA Ops:
  0.7 19.8 %all_gather.96 = bf16[6,32768]{1,0:T(8,128)(2,1)S(1)} all-gather(bf16[6,2048]{1,0:T(8,128)(2,1)} %param.69), channel_id=1, replica_groups=mesh['section'=32,'neuron'=16] {'neuron'}, dimensions={1}, use_global_device_ids=true | all-gather | bytes 417792 | tf_op jit(solution)/shard_map/all_gather | solution.py:49
  21.8 16.3 %all_gather.97 = bf16[6,32768]{1,0:T(8,128)(2,1)S(1)} all-gather(bf16[6,2048]{1,0:T(8,128)(2,1)S(1)} %collective-permute-done), channel_id=1, replica_groups=mesh['section'=32,'neuron'=16] {'neuron'}, dimensions={1}, use_global_device_ids=true | all-gather | bytes 417792 | tf_op jit(solution)/shard_map/all_gather | solution.py:49
  38.8 16.8 %all_gather.98 = bf16[6,32768]{1,0:T(8,128)(2,1)S(1)} all-gather(bf16[6,2048]{1,0:T(8,128)(2,1)S(1)} %collective-permute-done.1), channel_id=1, replica_groups=mesh['section'=32,'neuron'=16] {'neuron'}, dimensions={1}, use_global_device_ids=true | all-gather | bytes 417792 | tf_op jit(solution)/shard_map/all_gather | solution.py:49
  56.3 16.3 %all_gather.99 = bf16[6,32768]{1,0:T(8,128)(2,1)S(1)} all-gather(bf16[6,2048]{1,0:T(8,128)(2,1)S(1)} %collective-permute-done.2), channel_id=1, replica_groups=mesh['section'=32,'neuron'=16] {'neuron'}, dimensions={1}, use_global_device_ids=true | all-gather | bytes 417792 | tf_op jit(solution)/shard_map/all_gather | solution.py:49
  73.3 16.8 %all_gather.100 = bf16[6,32768]{1,0:T(8,128)(2,1)S(1)} all-gather(bf16[6,2048]{1,0:T(8,128)(2,1)S(1)} %collective-permute-done.3), channel_id=1, replica_groups=mesh['section'=32,'neuron'=16] {'neuron'}, dimensions={1}, use_global_device_ids=true | all-gather | bytes 417792 | tf_op jit(solution)/shard_map/all_gather | solution.py:49
  90.8 16.3 %all_gather.101 = bf16[6,32768]{1,0:T(8,128)(2,1)S(1)} all-gather(bf16[6,2048]{1,0:T(8,128)(2,1)S(1)} %collective-permute-done.4), channel_id=1, replica_groups=mesh['section'=32,'neuron'=16] {'neuron'}, dimensions={1}, use_global_device_ids=true | all-gather | bytes 417792 | tf_op jit(solution)/shard_map/all_gather | solution.py:49
  107.8 16.8 %all_gather.102 = bf16[6,32768]{1,0:T(8,128)(2,1)S(1)} all-gather(bf16[6,2048]{1,0:T(8,128)(2,1)S(1)} %collective-permute-done.5), channel_id=1, replica_groups=mesh['section'=32,'neuron'=16] {'neuron'}, dimensions={1}, use_global_device_ids=true | all-gather | bytes 417792 | tf_op jit(solution)/shard_map/all_gather | solution.py:49
  125.3 16.3 %all_gather.103 = bf16[6,32768]{1,0:T(8,128)(2,1)S(1)} all-gather(bf16[6,2048]{1,0:T(8,128)(2,1)S(1)} %collective-permute-done.6), channel_id=1, replica_groups=mesh['section'=32,'neuron'=16] {'neuron'}, dimensions={1}, use_global_device_ids=true | all-gather | bytes 417792 | tf_op jit(solution)/shard_map/all_gather | solution.py:49
  142.3 17.3 %all_gather.104 = bf16[6,32768]{1,0:T(8,128)(2,1)S(1)} all-gather(bf16[6,2048]{1,0:T(8,128)(2,1)S(1)} %collective-permute-done.7), channel_id=1, replica_groups=mesh['section'=32,'neuron'=16] {'neuron'}, dimensions={1}, use_global_device_ids=true | all-gather | bytes 417792 | tf_op jit(solution)/shard_map/all_gather | solution.py:49
  177.3 16.8 %all_gather.106 = bf16[6,32768]{1,0:T(8,128)(2,1)S(1)} all-gather(bf16[6,2048]{1,0:T(8,128)(2,1)S(1)} %collective-permute-done.9), channel_id=1, replica_groups=mesh['section'=32,'neuron'=16] {'neuron'}, dimensions={1}, use_global_device_ids=true | all-gather | bytes 417792 | tf_op jit(solution)/shard_map/all_gather | solution.py:49
  194.8 16.3 %all_gather.107 = bf16[6,32768]{1,0:T(8,128)(2,1)S(1)} all-gather(bf16[6,2048]{1,0:T(8,128)(2,1)S(1)} %collective-permute-done.10), channel_id=1, replica_groups=mesh['section'=32,'neuron'=16] {'neuron'}, dimensions={1}, use_global_device_ids=true | all-gather | bytes 417792 | tf_op jit(solution)/shard_map/all_gather | solution.py:49
  211.8 16.8 %all_gather.108 = bf16[6,32768]{1,0:T(8,128)(2,1)S(1)} all-gather(bf16[6,2048]{1,0:T(8,128)(2,1)S(1)} %collective-permute-done.11), channel_id=1, replica_groups=mesh['section'=32,'neuron'=16] {'neuron'}, dimensions={1}, use_global_device_ids=true | all-gather | bytes 417792 | tf_op jit(solution)/shard_map/all_gather | solution.py:49
  229.3 16.3 %all_gather.109 = bf16[6,32768]{1,0:T(8,128)(2,1)S(1)} all-gather(bf16[6,2048]{1,0:T(8,128)(2,1)S(1)} %collective-permute-done.12), channel_id=1, replica_groups=mesh['section'=32,'neuron'=16] {'neuron'}, dimensions={1}, use_global_device_ids=true | all-gather | bytes 417792 | tf_op jit(solution)/shard_map/all_gather | solution.py:49
  246.3 16.8 %all_gather.110 = bf16[6,32768]{1,0:T(8,128)(2,1)S(1)} all-gather(bf16[6,2048]{1,0:T(8,128)(2,1)S(1)} %collective-permute-done.13), channel_id=1, replica_groups=mesh['section'=32,'neuron'=16] {'neuron'}, dimensions={1}, use_global_device_ids=true | all-gather | bytes 417792 | tf_op jit(solution)/shard_map/all_gather | solution.py:49
  263.8 16.3 %all_gather.111 = bf16[6,32768]{1,0:T(8,128)(2,1)S(1)} all-gather(bf16[6,2048]{1,0:T(8,128)(2,1)S(1)} %collective-permute-done.14), channel_id=1, replica_groups=mesh['section'=32,'neuron'=16] {'neuron'}, dimensions={1}, use_global_device_ids=true | all-gather | bytes 417792 | tf_op jit(solution)/shard_map/all_gather | solution.py:49
  280.8 16.8 %all_gather.112 = bf16[6,32768]{1,0:T(8,128)(2,1)S(1)} all-gather(bf16[6,2048]{1,0:T(8,128)(2,1)S(1)} %collective-permute-done.15), channel_id=1, replica_groups=mesh['section'=32,'neuron'=16] {'neuron'}, dimensions={1}, use_global_device_ids=true | all-gather | bytes 417792 | tf_op jit(solution)/shard_map/all_gather | solution.py:49
  298.5 16.3 %all_gather.113 = bf16[6,32768]{1,0:T(8,128)(2,1)S(1)} all-gather(bf16[6,2048]{1,0:T(8,128)(2,1)S(1)} %collective-permute-done.16), channel_id=1, replica_groups=mesh['section'=32,'neuron'=16] {'neuron'}, dimensions={1}, use_global_device_ids=true | all-gather | bytes 417792 | tf_op jit(solution)/shard_map/all_gather | solution.py:49
  315.5 16.8 %all_gather.114 = bf16[6,32768]{1,0:T(8,128)(2,1)S(1)} all-gather(bf16[6,2048]{1,0:T(8,128)(2,1)S(1)} %collective-permute-done.17), channel_id=1, replica_groups=mesh['section'=32,'neuron'=16] {'neuron'}, dimensions={1}, use_global_device_ids=true | all-gather | bytes 417792 | tf_op jit(solution)/shard_map/all_gather | solution.py:49
  333.0 16.3 %all_gather.115 = bf16[6,32768]{1,0:T(8,128)(2,1)S(1)} all-gather(bf16[6,2048]{1,0:T(8,128)(2,1)S(1)} %collective-permute-done.18), channel_id=1, replica_groups=mesh['section'=32,'neuron'=16] {'neuron'}, dimensions={1}, use_global_device_ids=true | all-gather | bytes 417792 | tf_op jit(solution)/shard_map/all_gather | solution.py:49
  350.0 16.8 %all_gather.116 = bf16[6,32768]{1,0:T(8,128)(2,1)S(1)} all-gather(bf16[6,2048]{1,0:T(8,128)(2,1)S(1)} %collective-permute-done.19), channel_id=1, replica_groups=mesh['section'=32,'neuron'=16] {'neuron'}, dimensions={1}, use_global_device_ids=true | all-gather | bytes 417792 | tf_op jit(solution)/shard_map/all_gather | solution.py:49
  367.5 16.3 %all_gather.117 = bf16[6,32768]{1,0:T(8,128)(2,1)S(1)} all-gather(bf16[6,2048]{1,0:T(8,128)(2,1)S(1)} %collective-permute-done.20), channel_id=1, replica_groups=mesh['section'=32,'neuron'=16] {'neuron'}, dimensions={1}, use_global_device_ids=true | all-gather | bytes 417792 | tf_op jit(solution)/shard_map/all_gather | solution.py:49
  384.5 16.8 %all_gather.118 = bf16[6,32768]{1,0:T(8,128)(2,1)S(1)} all-gather(bf16[6,2048]{1,0:T(8,128)(2,1)S(1)} %collective-permute-done.21), channel_id=1, replica_groups=mesh['section'=32,'neuron'=16] {'neuron'}, dimensions={1}, use_global_device_ids=true | all-gather | bytes 417792 | tf_op jit(solution)/shard_map/all_gather | solution.py:49
  402.0 16.3 %all_gather.119 = bf16[6,32768]{1,0:T(8,128)(2,1)S(1)} all-gather(bf16[6,2048]{1,0:T(8,128)(2,1)S(1)} %collective-permute-done.22), channel_id=1, replica_groups=mesh['section'=32,'neuron'=16] {'neuron'}, dimensions={1}, use_global_device_ids=true | all-gather | bytes 417792 | tf_op jit(solution)/shard_map/all_gather | solution.py:49
  419.0 16.8 %all_gather.120 = bf16[6,32768]{1,0:T(8,128)(2,1)S(1)} all-gather(bf16[6,2048]{1,0:T(8,128)(2,1)S(1)} %collective-permute-done.23), channel_id=1, replica_groups=mesh['section'=32,'neuron'=16] {'neuron'}, dimensions={1}, use_global_device_ids=true | all-gather | bytes 417792 | tf_op jit(solution)/shard_map/all_gather | solution.py:49
  436.7 16.3 %all_gather.121 = bf16[6,32768]{1,0:T(8,128)(2,1)S(1)} all-gather(bf16[6,2048]{1,0:T(8,128)(2,1)S(1)} %collective-permute-done.24), channel_id=1, replica_groups=mesh['section'=32,'neuron'=16] {'neuron'}, dimensions={1}, use_global_device_ids=true | all-gather | bytes 417792 | tf_op jit(solution)/shard_map/all_gather | solution.py:49
  453.7 16.8 %all_gather.122 = bf16[6,32768]{1,0:T(8,128)(2,1)S(1)} all-gather(bf16[6,2048]{1,0:T(8,128)(2,1)S(1)} %collective-permute-done.25), channel_id=1, replica_groups=mesh['section'=32,'neuron'=16] {'neuron'}, dimensions={1}, use_global_device_ids=true | all-gather | bytes 417792 | tf_op jit(solution)/shard_map/all_gather | solution.py:49
  471.2 16.3 %all_gather.123 = bf16[6,32768]{1,0:T(8,128)(2,1)S(1)} all-gather(bf16[6,2048]{1,0:T(8,128)(2,1)S(1)} %collective-permute-done.26), channel_id=1, replica_groups=mesh['section'=32,'neuron'=16] {'neuron'}, dimensions={1}, use_global_device_ids=true | all-gather | bytes 417792 | tf_op jit(solution)/shard_map/all_gather | solution.py:49
  488.2 16.8 %all_gather.124 = bf16[6,32768]{1,0:T(8,128)(2,1)S(1)} all-gather(bf16[6,2048]{1,0:T(8,128)(2,1)S(1)} %collective-permute-done.27), channel_id=1, replica_groups=mesh['section'=32,'neuron'=16] {'neuron'}, dimensions={1}, use_global_device_ids=true | all-gather | bytes 417792 | tf_op jit(solution)/shard_map/all_gather | solution.py:49
  505.7 16.3 %all_gather.125 = bf16[6,32768]{1,0:T(8,128)(2,1)S(1)} all-gather(bf16[6,2048]{1,0:T(8,128)(2,1)S(1)} %collective-permute-done.28), channel_id=1, replica_groups=mesh['section'=32,'neuron'=16] {'neuron'}, dimensions={1}, use_global_device_ids=true | all-gather | bytes 417792 | tf_op jit(solution)/shard_map/all_gather | solution.py:49
  522.7 16.8 %all_gather.126 = bf16[6,32768]{1,0:T(8,128)(2,1)S(1)} all-gather(bf16[6,2048]{1,0:T(8,128)(2,1)S(1)} %collective-permute-done.29), channel_id=1, replica_groups=mesh['section'=32,'neuron'=16] {'neuron'}, dimensions={1}, use_global_device_ids=true | all-gather | bytes 417792 | tf_op jit(solution)/shard_map/all_gather | solution.py:49
  540.8 266.8 %collective-permute-done.30 = bf16[6,2048]{1,0:T(8,128)(2,1)S(1)} collective-permute-done((bf16[6,2048]{1,0:T(8,128)(2,1)S(1)}, bf16[6,2048]{1,0:T(8,128)(2,1)S(1)}, u32[]{:S(2)}, u32[]{:S(2)}) %collective-permute-start.30) | collective-permute-done | bytes 24608 | tf_op jit(solution)/shard_map/ppermute | solution.py:55
  807.6 17.9 %all_gather.127 = bf16[6,32768]{1,0:T(8,128)(2,1)S(1)} all-gather(bf16[6,2048]{1,0:T(8,128)(2,1)S(1)} %collective-permute-done.30), channel_id=1, replica_groups=mesh['section'=32,'neuron'=16] {'neuron'}, dimensions={1}, use_global_device_ids=true | all-gather | bytes 417792 | tf_op jit(solution)/shard_map/all_gather | solution.py:49
  (134 shorter events, 49.7 us)
Async XLA Ops:
  21.1 0.7 collective-permute-start
  38.2 0.7 collective-permute-start.1
  55.6 0.7 collective-permute-start.2
  72.7 0.7 collective-permute-start.3
  90.1 0.7 collective-permute-start.4
  107.2 0.7 collective-permute-start.5
  124.6 0.7 collective-permute-start.6
  141.7 0.7 collective-permute-start.7
  159.6 0.7 collective-permute-start.8
  176.6 0.7 collective-permute-start.9
  194.1 0.7 collective-permute-start.10
  211.1 0.7 collective-permute-start.11
  228.6 0.7 collective-permute-start.12
  245.6 0.7 collective-permute-start.13
  263.1 0.7 collective-permute-start.14
  280.1 0.7 collective-permute-start.15
  297.8 0.7 collective-permute-start.16
  314.8 0.7 collective-permute-start.17
  332.3 0.7 collective-permute-start.18
  349.3 0.7 collective-permute-start.19
  366.8 0.7 collective-permute-start.20
  383.8 0.7 collective-permute-start.21
  401.3 0.7 collective-permute-start.22
  418.3 0.7 collective-permute-start.23
  436.0 0.7 collective-permute-start.24
  453.0 0.7 collective-permute-start.25
  470.5 0.7 collective-permute-start.26
  487.5 0.7 collective-permute-start.27
  505.0 0.7 collective-permute-start.28
  522.0 0.7 collective-permute-start.29
  539.5 268.1 %collective-permute-start.30 = (bf16[6,2048]{1,0:T(8,128)(2,1)S(1)}, bf16[6,2048]{1,0:T(8,128)(2,1)S(1)}, u32[]{:S(2)}, u32[]{:S(2)}) collective-permute-start(bf16[6,2048]{1,0:T(8,128)(2,1)S(1)} %get-tuple-element.515), channel_id=1, source_target_pairs={{480,496},{481,497},{482,498},{483,499},{484,500},{485,501},{486,5... | collective-permute-start | bytes 73736 | tf_op jit(solution)/shard_map/ppermute | solution.py:55
where the time goes:
time: 841 us; the launch traced here: 832 us
  blocking collectives  535 us (64%)
  waiting for transfers between devices  267 us (32%)
  starting transfers between devices  20.9 us (2%)
    all_gather x32, blocking collectives, step(): gathered = lax.all_gather(current, 'neuron', axis=1, tiled=True)  535 us
    ppermute x31, waiting for transfers between devices, step(): return (lax.ppermute(result, 'section', route), collected)  267 us
    ppermute x31, starting transfers between devices, step(): return (lax.ppermute(result, 'section', route), collected)  20.9 us
  transfers between devices with their start and end apart: 31, of which 1 were waited for; matrix products, arithmetic and copies ran while one was open for 0% of the time, Pallas kernels for 0%

commit v1 on v0

--- a/solution.py
+++ b/solution.py
@@ -48,7 +48,7 @@
     def step(step_num, current, collected, route):
         gathered = lax.all_gather(current, "neuron", axis=1, tiled=True)
         active = section_pos == step_num
-        result = lax.cond(active, compute, empty, gathered)
+        result = compute(gathered)
         collected = jnp.where(active, result, collected)
         if route is None:
             return result, collected

time: 841 us -> 820 us (0.975)
  waiting for transfers between devices: 267 us -> 108 us
  matrix products: 3.73 us -> 117 us
  local copies, waits for them, and re-layouts: 0.87 us -> 25 us
    ppermute x31, waiting for transfers between devices: 267 us -> 108 us  [step(): return (lax.ppermute(result, 'section', route), collected)]
    dot_general x1 -> x32, matrix products: 3.37 us -> 108 us  [layer_apply(): jnp.einsum('msk,skj->msj', picked, weight_tiles[0], preferred_element_typ...]
    gather x1 -> x32, local copies, waits for them, and re-layouts: 0.69 us -> 23.8 us  [layer_apply(): picked = shaped.at[:, source].get(mode='promise_in_bounds')]
    dot_general x1 -> x32, matrix products: 0.36 us -> 9.48 us  [layer_apply(): jnp.einsum('msj,sc->mcj', partial_value, selector, precision=lax.Precisio...]
where the time goes in v1:
time: 820 us; the launch traced here: 810 us
  blocking collectives  535 us (65%)
  matrix products  117 us (14%)
  waiting for transfers between devices  108 us (13%)
  local copies, waits for them, and re-layouts  25 us (3%)
  starting transfers between devices  21.2 us (3%)
    all_gather x32, blocking collectives, step(): gathered = lax.all_gather(current, 'neuron', axis=1, tiled=True)  535 us
    dot_general x32, matrix products, layer_apply(): jnp.einsum('msk,skj->msj', picked, weight_tiles[0], preferred_element_typ...  108 us
    ppermute x31, waiting for transfers between devices, step(): return (lax.ppermute(result, 'section', route), collected)  108 us
    gather x32, local copies, waits for them, and re-layouts, layer_apply(): picked = shaped.at[:, source].get(mode='promise_in_bounds')  23.8 us
    ppermute x31, starting transfers between devices, step(): return (lax.ppermute(result, 'section', route), collected)  21.2 us
  transfers between devices with their start and end apart: 31, of which 1 were waited for; matrix products, arithmetic and copies ran while one was open for 0% of the time, Pallas kernels for 0%

profile of v1, /device:TPU:455, one launch (start us, length us, event | category | flops | bytes accessed | tf_op | source)
XLA Modules:
  0.0 809.9 jit_solution(16794483580277421957)
XLA Ops:
  0.7 19.8 %all_gather.96 = bf16[6,32768]{1,0:T(8,128)(2,1)S(1)} all-gather(bf16[6,2048]{1,0:T(8,128)(2,1)} %param.5), channel_id=1, replica_groups=mesh['section'=32,'neuron'=16] {'neuron'}, dimensions={1}, use_global_device_ids=true | all-gather | bytes 417792 | tf_op jit(solution)/shard_map/all_gather | solution.py:49
  26.2 16.3 %all_gather.97 = bf16[6,32768]{1,0:T(8,128)(2,1)S(1)} all-gather(bf16[6,2048]{1,0:T(8,128)(2,1)S(1)} %collective-permute-done), channel_id=1, replica_groups=mesh['section'=32,'neuron'=16] {'neuron'}, dimensions={1}, use_global_device_ids=true | all-gather | bytes 417792 | tf_op jit(solution)/shard_map/all_gather | solution.py:49
  47.7 16.8 %all_gather.98 = bf16[6,32768]{1,0:T(8,128)(2,1)S(1)} all-gather(bf16[6,2048]{1,0:T(8,128)(2,1)S(1)} %collective-permute-done.1), channel_id=1, replica_groups=mesh['section'=32,'neuron'=16] {'neuron'}, dimensions={1}, use_global_device_ids=true | all-gather | bytes 417792 | tf_op jit(solution)/shard_map/all_gather | solution.py:49
  69.7 16.3 %all_gather.99 = bf16[6,32768]{1,0:T(8,128)(2,1)S(1)} all-gather(bf16[6,2048]{1,0:T(8,128)(2,1)S(1)} %collective-permute-done.2), channel_id=1, replica_groups=mesh['section'=32,'neuron'=16] {'neuron'}, dimensions={1}, use_global_device_ids=true | all-gather | bytes 417792 | tf_op jit(solution)/shard_map/all_gather | solution.py:49
  91.2 16.8 %all_gather.100 = bf16[6,32768]{1,0:T(8,128)(2,1)S(1)} all-gather(bf16[6,2048]{1,0:T(8,128)(2,1)S(1)} %collective-permute-done.3), channel_id=1, replica_groups=mesh['section'=32,'neuron'=16] {'neuron'}, dimensions={1}, use_global_device_ids=true | all-gather | bytes 417792 | tf_op jit(solution)/shard_map/all_gather | solution.py:49
  113.2 16.3 %all_gather.101 = bf16[6,32768]{1,0:T(8,128)(2,1)S(1)} all-gather(bf16[6,2048]{1,0:T(8,128)(2,1)S(1)} %collective-permute-done.4), channel_id=1, replica_groups=mesh['section'=32,'neuron'=16] {'neuron'}, dimensions={1}, use_global_device_ids=true | all-gather | bytes 417792 | tf_op jit(solution)/shard_map/all_gather | solution.py:49
  134.7 16.8 %all_gather.102 = bf16[6,32768]{1,0:T(8,128)(2,1)S(1)} all-gather(bf16[6,2048]{1,0:T(8,128)(2,1)S(1)} %collective-permute-done.5), channel_id=1, replica_groups=mesh['section'=32,'neuron'=16] {'neuron'}, dimensions={1}, use_global_device_ids=true | all-gather | bytes 417792 | tf_op jit(solution)/shard_map/all_gather | solution.py:49
  156.7 16.3 %all_gather.103 = bf16[6,32768]{1,0:T(8,128)(2,1)S(1)} all-gather(bf16[6,2048]{1,0:T(8,128)(2,1)S(1)} %collective-permute-done.6), channel_id=1, replica_groups=mesh['section'=32,'neuron'=16] {'neuron'}, dimensions={1}, use_global_device_ids=true | all-gather | bytes 417792 | tf_op jit(solution)/shard_map/all_gather | solution.py:49
  178.2 17.0 %all_gather.104 = bf16[6,32768]{1,0:T(8,128)(2,1)S(1)} all-gather(bf16[6,2048]{1,0:T(8,128)(2,1)S(1)} %collective-permute-done.7), channel_id=1, replica_groups=mesh['section'=32,'neuron'=16] {'neuron'}, dimensions={1}, use_global_device_ids=true | all-gather | bytes 417792 | tf_op jit(solution)/shard_map/all_gather | solution.py:49
  200.4 16.3 %all_gather.105 = bf16[6,32768]{1,0:T(8,128)(2,1)S(1)} all-gather(bf16[6,2048]{1,0:T(8,128)(2,1)S(1)} %collective-permute-done.8), channel_id=1, replica_groups=mesh['section'=32,'neuron'=16] {'neuron'}, dimensions={1}, use_global_device_ids=true | all-gather | bytes 417792 | tf_op jit(solution)/shard_map/all_gather | solution.py:49
  221.9 16.8 %all_gather.106 = bf16[6,32768]{1,0:T(8,128)(2,1)S(1)} all-gather(bf16[6,2048]{1,0:T(8,128)(2,1)S(1)} %collective-permute-done.9), channel_id=1, replica_groups=mesh['section'=32,'neuron'=16] {'neuron'}, dimensions={1}, use_global_device_ids=true | all-gather | bytes 417792 | tf_op jit(solution)/shard_map/all_gather | solution.py:49
  243.9 16.3 %all_gather.107 = bf16[6,32768]{1,0:T(8,128)(2,1)S(1)} all-gather(bf16[6,2048]{1,0:T(8,128)(2,1)S(1)} %collective-permute-done.10), channel_id=1, replica_groups=mesh['section'=32,'neuron'=16] {'neuron'}, dimensions={1}, use_global_device_ids=true | all-gather | bytes 417792 | tf_op jit(solution)/shard_map/all_gather | solution.py:49
  265.4 16.8 %all_gather.108 = bf16[6,32768]{1,0:T(8,128)(2,1)S(1)} all-gather(bf16[6,2048]{1,0:T(8,128)(2,1)S(1)} %collective-permute-done.11), channel_id=1, replica_groups=mesh['section'=32,'neuron'=16] {'neuron'}, dimensions={1}, use_global_device_ids=true | all-gather | bytes 417792 | tf_op jit(solution)/shard_map/all_gather | solution.py:49
  287.4 16.3 %all_gather.109 = bf16[6,32768]{1,0:T(8,128)(2,1)S(1)} all-gather(bf16[6,2048]{1,0:T(8,128)(2,1)S(1)} %collective-permute-done.12), channel_id=1, replica_groups=mesh['section'=32,'neuron'=16] {'neuron'}, dimensions={1}, use_global_device_ids=true | all-gather | bytes 417792 | tf_op jit(solution)/shard_map/all_gather | solution.py:49
  308.9 16.8 %all_gather.110 = bf16[6,32768]{1,0:T(8,128)(2,1)S(1)} all-gather(bf16[6,2048]{1,0:T(8,128)(2,1)S(1)} %collective-permute-done.13), channel_id=1, replica_groups=mesh['section'=32,'neuron'=16] {'neuron'}, dimensions={1}, use_global_device_ids=true | all-gather | bytes 417792 | tf_op jit(solution)/shard_map/all_gather | solution.py:49
  330.9 16.3 %all_gather.111 = bf16[6,32768]{1,0:T(8,128)(2,1)S(1)} all-gather(bf16[6,2048]{1,0:T(8,128)(2,1)S(1)} %collective-permute-done.14), channel_id=1, replica_groups=mesh['section'=32,'neuron'=16] {'neuron'}, dimensions={1}, use_global_device_ids=true | all-gather | bytes 417792 | tf_op jit(solution)/shard_map/all_gather | solution.py:49
  352.3 17.0 %all_gather.112 = bf16[6,32768]{1,0:T(8,128)(2,1)S(1)} all-gather(bf16[6,2048]{1,0:T(8,128)(2,1)S(1)} %collective-permute-done.15), channel_id=1, replica_groups=mesh['section'=32,'neuron'=16] {'neuron'}, dimensions={1}, use_global_device_ids=true | all-gather | bytes 417792 | tf_op jit(solution)/shard_map/all_gather | solution.py:49
  374.4 16.3 %all_gather.113 = bf16[6,32768]{1,0:T(8,128)(2,1)S(1)} all-gather(bf16[6,2048]{1,0:T(8,128)(2,1)S(1)} %collective-permute-done.16), channel_id=1, replica_groups=mesh['section'=32,'neuron'=16] {'neuron'}, dimensions={1}, use_global_device_ids=true | all-gather | bytes 417792 | tf_op jit(solution)/shard_map/all_gather | solution.py:49
  395.8 16.8 %all_gather.114 = bf16[6,32768]{1,0:T(8,128)(2,1)S(1)} all-gather(bf16[6,2048]{1,0:T(8,128)(2,1)S(1)} %collective-permute-done.17), channel_id=1, replica_groups=mesh['section'=32,'neuron'=16] {'neuron'}, dimensions={1}, use_global_device_ids=true | all-gather | bytes 417792 | tf_op jit(solution)/shard_map/all_gather | solution.py:49
  417.7 16.3 %all_gather.115 = bf16[6,32768]{1,0:T(8,128)(2,1)S(1)} all-gather(bf16[6,2048]{1,0:T(8,128)(2,1)S(1)} %collective-permute-done.18), channel_id=1, replica_groups=mesh['section'=32,'neuron'=16] {'neuron'}, dimensions={1}, use_global_device_ids=true | all-gather | bytes 417792 | tf_op jit(solution)/shard_map/all_gather | solution.py:49
  439.1 16.8 %all_gather.116 = bf16[6,32768]{1,0:T(8,128)(2,1)S(1)} all-gather(bf16[6,2048]{1,0:T(8,128)(2,1)S(1)} %collective-permute-done.19), channel_id=1, replica_groups=mesh['section'=32,'neuron'=16] {'neuron'}, dimensions={1}, use_global_device_ids=true | all-gather | bytes 417792 | tf_op jit(solution)/shard_map/all_gather | solution.py:49
  460.9 16.3 %all_gather.117 = bf16[6,32768]{1,0:T(8,128)(2,1)S(1)} all-gather(bf16[6,2048]{1,0:T(8,128)(2,1)S(1)} %collective-permute-done.20), channel_id=1, replica_groups=mesh['section'=32,'neuron'=16] {'neuron'}, dimensions={1}, use_global_device_ids=true | all-gather | bytes 417792 | tf_op jit(solution)/shard_map/all_gather | solution.py:49
  482.3 16.8 %all_gather.118 = bf16[6,32768]{1,0:T(8,128)(2,1)S(1)} all-gather(bf16[6,2048]{1,0:T(8,128)(2,1)S(1)} %collective-permute-done.21), channel_id=1, replica_groups=mesh['section'=32,'neuron'=16] {'neuron'}, dimensions={1}, use_global_device_ids=true | all-gather | bytes 417792 | tf_op jit(solution)/shard_map/all_gather | solution.py:49
  504.2 16.3 %all_gather.119 = bf16[6,32768]{1,0:T(8,128)(2,1)S(1)} all-gather(bf16[6,2048]{1,0:T(8,128)(2,1)S(1)} %collective-permute-done.22), channel_id=1, replica_groups=mesh['section'=32,'neuron'=16] {'neuron'}, dimensions={1}, use_global_device_ids=true | all-gather | bytes 417792 | tf_op jit(solution)/shard_map/all_gather | solution.py:49
  525.6 17.1 %all_gather.120 = bf16[6,32768]{1,0:T(8,128)(2,1)S(1)} all-gather(bf16[6,2048]{1,0:T(8,128)(2,1)S(1)} %collective-permute-done.23), channel_id=1, replica_groups=mesh['section'=32,'neuron'=16] {'neuron'}, dimensions={1}, use_global_device_ids=true | all-gather | bytes 417792 | tf_op jit(solution)/shard_map/all_gather | solution.py:49
  547.7 16.3 %all_gather.121 = bf16[6,32768]{1,0:T(8,128)(2,1)S(1)} all-gather(bf16[6,2048]{1,0:T(8,128)(2,1)S(1)} %collective-permute-done.24), channel_id=1, replica_groups=mesh['section'=32,'neuron'=16] {'neuron'}, dimensions={1}, use_global_device_ids=true | all-gather | bytes 417792 | tf_op jit(solution)/shard_map/all_gather | solution.py:49
  569.1 16.8 %all_gather.122 = bf16[6,32768]{1,0:T(8,128)(2,1)S(1)} all-gather(bf16[6,2048]{1,0:T(8,128)(2,1)S(1)} %collective-permute-done.25), channel_id=1, replica_groups=mesh['section'=32,'neuron'=16] {'neuron'}, dimensions={1}, use_global_device_ids=true | all-gather | bytes 417792 | tf_op jit(solution)/shard_map/all_gather | solution.py:49
  590.9 16.3 %all_gather.123 = bf16[6,32768]{1,0:T(8,128)(2,1)S(1)} all-gather(bf16[6,2048]{1,0:T(8,128)(2,1)S(1)} %collective-permute-done.26), channel_id=1, replica_groups=mesh['section'=32,'neuron'=16] {'neuron'}, dimensions={1}, use_global_device_ids=true | all-gather | bytes 417792 | tf_op jit(solution)/shard_map/all_gather | solution.py:49
  612.3 16.8 %all_gather.124 = bf16[6,32768]{1,0:T(8,128)(2,1)S(1)} all-gather(bf16[6,2048]{1,0:T(8,128)(2,1)S(1)} %collective-permute-done.27), channel_id=1, replica_groups=mesh['section'=32,'neuron'=16] {'neuron'}, dimensions={1}, use_global_device_ids=true | all-gather | bytes 417792 | tf_op jit(solution)/shard_map/all_gather | solution.py:49
  655.6 16.8 %all_gather.126 = bf16[6,32768]{1,0:T(8,128)(2,1)S(1)} all-gather(bf16[6,2048]{1,0:T(8,128)(2,1)S(1)} %collective-permute-done.29), channel_id=1, replica_groups=mesh['section'=32,'neuron'=16] {'neuron'}, dimensions={1}, use_global_device_ids=true | all-gather | bytes 417792 | tf_op jit(solution)/shard_map/all_gather | solution.py:49
  679.0 107.4 %collective-permute-done.30 = bf16[6,2048]{1,0:T(8,128)(2,1)S(1)} collective-permute-done((bf16[6,2048]{1,0:T(8,128)(2,1)S(1)}, bf16[6,2048]{1,0:T(8,128)(2,1)S(1)}, u32[]{:S(2)}, u32[]{:S(2)}) %collective-permute-start.30) | collective-permute-done | bytes 24608 | tf_op jit(solution)/shard_map/ppermute | solution.py:55
  786.5 17.9 %all_gather.127 = bf16[6,32768]{1,0:T(8,128)(2,1)S(1)} all-gather(bf16[6,2048]{1,0:T(8,128)(2,1)S(1)} %collective-permute-done.30), channel_id=1, replica_groups=mesh['section'=32,'neuron'=16] {'neuron'}, dimensions={1}, use_global_device_ids=true | all-gather | bytes 417792 | tf_op jit(solution)/shard_map/all_gather | solution.py:49
  (216 shorter events, 181.3 us)
Async XLA Ops:
  0.7 41.9 %copy-start.1 = (s32[1024]{0:T(1024)}, s32[1024]{0:T(1024)S(1)}, u32[]{:S(2)}) copy-start(s32[1024]{0:T(1024)S(1)} %pad_clamp_fusion) | copy-start | bytes 12292
  25.5 0.7 collective-permute-start
  47.0 0.7 collective-permute-start.1
  69.0 0.7 collective-permute-start.2
  90.5 0.7 collective-permute-start.3
  112.5 0.7 collective-permute-start.4
  134.0 0.7 collective-permute-start.5
  156.0 0.7 collective-permute-start.6
  177.5 0.7 collective-permute-start.7
  199.7 0.7 collective-permute-start.8
  221.2 0.7 collective-permute-start.9
  243.2 0.7 collective-permute-start.10
  264.7 0.7 collective-permute-start.11
  286.7 0.7 collective-permute-start.12
  308.2 0.7 collective-permute-start.13
  330.2 0.7 collective-permute-start.14
  351.6 0.7 collective-permute-start.15
  373.7 0.7 collective-permute-start.16
  395.1 0.7 collective-permute-start.17
  417.0 0.7 collective-permute-start.18
  438.4 0.7 collective-permute-start.19
  460.2 0.7 collective-permute-start.20
  481.6 0.7 collective-permute-start.21
  503.5 0.7 collective-permute-start.22
  524.9 0.7 collective-permute-start.23
  547.0 0.7 collective-permute-start.24
  568.4 0.7 collective-permute-start.25
  590.3 0.7 collective-permute-start.26
  611.7 0.7 collective-permute-start.27
  633.5 0.7 collective-permute-start.28
  654.9 0.7 collective-permute-start.29
  676.8 109.7 %collective-permute-start.30 = (bf16[6,2048]{1,0:T(8,128)(2,1)S(1)}, bf16[6,2048]{1,0:T(8,128)(2,1)S(1)}, u32[]{:S(2)}, u32[]{:S(2)}) collective-permute-start(bf16[6,2048]{1,0:T(8,128)(2,1)S(1)} %bitcast.647), channel_id=1, source_target_pairs={{480,496},{481,497},{482,498},{483,499},{484,500},{485,501},{486,5... | collective-permute-start | bytes 73736 | tf_op jit(solution)/shard_map/ppermute | solution.py:55
  (2 other events, 64.6 us)
